TPU v7x, 32 devices: a whole 2x2x4 slice. The times are simulated.
32 devices in a mesh: seq: 8 (over z, y), head: 4 (over x, core).
Axes of the slice: x: 2, y: 2, z: 4, core: 2. Of those that a mesh axis runs over, the one named last changes fastest.
Arguments:
- projected: bfloat16 [1024, 3, 4096], P('seq', None, 'head'), may hold values from -8 to 8
- destination: int32 [1024], P('seq'), may hold values from 0 to 1023, as said below
- doc_lengths: int32 [4], replicated, may hold values from 1 to 512, 1024 in all
- random_blocks: int32 [8, 3], replicated, may hold values from 0 to 7, as said below
- global_owner: int32 [8], replicated, may hold values from 0 to 7, as said below
- out_weight: bfloat16 [4096, 4096], P('head'), may hold values from -0.09375 to 0.09375
Outputs:
- attended: bfloat16 [1024, 4096], P(('seq', 'head'))
Inputs may be any that keep to these rules, and one draw needn't show every extreme that they name: Each packed position appears exactly once. Of the rows of one device (one index of seq, 128 rows), at most 32 have destinations owned by one owner (destination // 128), and in every draw some device sends exactly 32 rows to some owner. The owner (index) of random_blocks[b, r] lies at most 2 owners away from the owner of block b, counted cyclically over the owners. `global_owner`: each owner appears exactly once.
All inputs are finite; a program needn't handle non-finite values.
Results may differ from a plain program's by a relative error of at most 0.015.
Values may be sent and summed in bfloat16 or wider, within the bound.
No kernel may reach another device: no remote copies, remote signals or barrier semaphores. Data moves between devices by JAX's collectives and lax.ppermute only.
A program may use at most 128 MiB of HBM per device.

v0:
```python
import math
import jax
import jax.numpy as jnp
from jax import lax
from jax.sharding import PartitionSpec as P

HD = 128
BLK = 128
R = 3
RDEV = 2
big_negative = -1e30


def from_behind(block, axis, distance):
    devices = range(lax.axis_size(axis))
    route = [((i - distance) % len(devices), i) for i in devices]
    return lax.ppermute(block, axis, route)


def from_root(x, axis, root):
    mine = lax.axis_index(axis) == root
    return lax.psum(jnp.where(mine, x, jnp.zeros_like(x)), axis)


def combined_all(x, axis, combine):
    everything = jax.tree.map(lambda part: lax.all_gather(part, axis), x)
    first = jax.tree.map(lambda part: part[0], everything)

    def step(k, so_far):
        return combine(so_far, jax.tree.map(lambda part: part[k], everything))

    return lax.fori_loop(1, lax.axis_size(axis), step, first)


def segment_of(positions, bounds):
    return jnp.sum((bounds[None, :] <= positions[:, None]).astype(jnp.int32), axis=1)


def combine_parts(left_part, right_part):
    top_left, total_left, accum_left = left_part
    top_right, total_right, accum_right = right_part
    row_peak = jnp.maximum(top_left, top_right)
    factor_left = jnp.exp(top_left - row_peak)
    factor_right = jnp.exp(top_right - row_peak)
    return (
        row_peak,
        total_left * factor_left + total_right * factor_right,
        accum_left * factor_left[:, :, None] + accum_right * factor_right[:, :, None],
    )


def shards_ring(projected, destination, doc_lengths, random_blocks, global_owner, out_weight):
    owners = lax.axis_size("seq")
    own_index = lax.axis_index("seq")
    tok_dev = projected.shape[0]
    columns = projected.shape[2]
    heads_here = columns // HD
    per_dev = tok_dev // BLK
    blocks_all = owners * per_dev
    capacity = 2 * (tok_dev // owners)
    score_scale = 1.0 / math.sqrt(HD)
    target_owner = destination // tok_dev
    onehot = (target_owner[:, None] == jnp.arange(owners, dtype=jnp.int32)[None, :]).astype(
        jnp.int32
    )
    before = jnp.cumsum(onehot, axis=0) - onehot
    slot_rank = jnp.sum(before * onehot, axis=1)
    outgoing = (
        jnp.zeros((owners, capacity, 3, columns), projected.dtype)
        .at[target_owner, slot_rank]
        .set(projected)
    )
    slots = (
        jnp.full((owners, capacity), -1, jnp.int32)
        .at[target_owner, slot_rank]
        .set(destination % tok_dev)
    )
    incoming, landing = (
        lax.all_to_all(outgoing, "seq", split_axis=0, concat_axis=0, tiled=True),
        lax.all_to_all(slots, "seq", split_axis=0, concat_axis=0, tiled=True),
    )
    landing = landing.reshape(-1)
    landing = jnp.where(landing >= 0, landing, tok_dev)
    routed = (
        jnp.zeros((tok_dev, 3, columns), projected.dtype)
        .at[landing]
        .set(incoming.reshape(owners * capacity, 3, columns), mode="drop")
    )
    keyval = routed[:, 1:, :]
    fetched = {0: keyval}
    offsets = list(range(-RDEV, 0)) + list(range(1, RDEV + 1))
    for offset in offsets:
        fetched[offset] = from_behind(keyval, "seq", -offset)
    band_blocks = jnp.stack([fetched[offset] for offset in range(-RDEV, RDEV + 1)])
    block_ids = own_index * per_dev + jnp.arange(per_dev, dtype=jnp.int32)
    local_pick = jnp.arange(per_dev, dtype=jnp.int32) + RDEV * per_dev
    window_pick = local_pick[:, None] + jnp.arange(-1, 2, dtype=jnp.int32)[None, :]
    chosen_rand = lax.dynamic_slice_in_dim(random_blocks, own_index * per_dev, per_dev, 0)
    away_dev = (chosen_rand // per_dev - own_index) % owners
    away_dev = jnp.where(away_dev > owners // 2, away_dev - owners, away_dev)
    rand_pick = (away_dev + RDEV) * per_dev + chosen_rand % per_dev
    block_picks = jnp.concatenate([window_pick, rand_pick], axis=1)
    gathered = jnp.take(band_blocks, block_picks, axis=0)
    near_keys = gathered[:, :, :, 0, :].reshape(per_dev, (3 + R) * BLK, heads_here, HD)
    near_values = gathered[:, :, :, 1, :].reshape(per_dev, (3 + R) * BLK, heads_here, HD)
    owner_dev = global_owner[0]
    global_rows = from_root(routed, "seq", owner_dev)
    glob_keys = global_rows[:, 1, :].reshape(tok_dev, heads_here, HD)
    glob_values = global_rows[:, 2, :].reshape(tok_dev, heads_here, HD)
    queries = routed[:, 0, :].reshape(per_dev, BLK, heads_here, HD)
    near_scores = (
        jnp.einsum("bqhd,bkhd->bhqk", queries, near_keys, preferred_element_type=jnp.float32)
        * score_scale
    )
    far_scores = (
        jnp.einsum("bqhd,khd->bhqk", queries, glob_keys, preferred_element_type=jnp.float32)
        * score_scale
    )
    bounds = jnp.cumsum(doc_lengths)
    query_pos = own_index * tok_dev + jnp.arange(tok_dev, dtype=jnp.int32)
    query_doc = segment_of(query_pos, bounds).reshape(per_dev, BLK)
    window_blocks = (block_ids[:, None] + jnp.arange(-1, 2, dtype=jnp.int32)[None, :]) % blocks_all
    key_pos = (
        window_blocks[:, :, None] * BLK + jnp.arange(BLK, dtype=jnp.int32)[None, None, :]
    ).reshape(-1)
    key_doc = segment_of(key_pos, bounds).reshape(per_dev, 3 * BLK)
    same_doc = query_doc[:, :, None] == key_doc[:, None, :]
    allowed = jnp.concatenate(
        [same_doc, jnp.ones((per_dev, BLK, R * BLK), dtype=jnp.bool_)], axis=2
    )
    near_scores = jnp.where(allowed[:, None], near_scores, big_negative)
    row_peak = jnp.maximum(jnp.max(near_scores, axis=3), jnp.max(far_scores, axis=3))
    near_exp = jnp.exp(near_scores - row_peak[..., None])
    far_exp = jnp.exp(far_scores - row_peak[..., None])
    denominator = jnp.sum(near_exp, axis=3) + jnp.sum(far_exp, axis=3)
    mixed_sum = jnp.einsum(
        "bhqk,bkhd->bqhd",
        near_exp.astype(jnp.bfloat16),
        near_values,
        preferred_element_type=jnp.float32,
    )
    mixed_sum = mixed_sum + jnp.einsum(
        "bhqk,khd->bqhd",
        far_exp.astype(jnp.bfloat16),
        glob_values,
        preferred_element_type=jnp.float32,
    )
    sparse = (mixed_sum / jnp.transpose(denominator, (0, 2, 1))[..., None]).reshape(
        tok_dev, columns
    )
    sparse = sparse.astype(jnp.bfloat16)
    glob_queries = global_rows[:, 0, :].reshape(tok_dev, heads_here, HD)
    local_keys = routed[:, 1, :].reshape(tok_dev, heads_here, HD)
    local_values = routed[:, 2, :].reshape(tok_dev, heads_here, HD).astype(jnp.float32)
    all_scores = (
        jnp.einsum("qhd,khd->hqk", glob_queries, local_keys, preferred_element_type=jnp.float32)
        * score_scale
    )
    local_peak = jnp.max(all_scores, axis=2)
    weights = jnp.exp(all_scores - local_peak[..., None])
    part_total = jnp.sum(weights, axis=2)
    part_accum = jnp.einsum("hqk,khd->hqd", weights, local_values, precision=lax.Precision.HIGHEST)
    peak_all, total_all, accum_all = combined_all(
        (local_peak, part_total, part_accum), "seq", combine_parts
    )
    glob_out = jnp.transpose(accum_all / total_all[..., None], (1, 0, 2)).reshape(tok_dev, columns)
    glob_out = glob_out.astype(jnp.bfloat16)
    attn_rows = jnp.where(own_index == owner_dev, glob_out, sparse)
    return lax.psum_scatter(
        jnp.dot(attn_rows, out_weight, preferred_element_type=jnp.float32).astype(jnp.bfloat16),
        "head",
        scatter_dimension=0,
        tiled=True,
    )


def gathered_plan(projected, destination, doc_lengths, random_blocks, global_owner, out_weight):
    owners = lax.axis_size("seq")
    own_index = lax.axis_index("seq")
    tok_dev = projected.shape[0]
    columns = projected.shape[2]
    heads_here = columns // HD
    tokens = owners * tok_dev
    blocks_all = tokens // BLK
    score_scale = 1.0 / math.sqrt(HD)
    everything = lax.all_gather(projected, "seq", tiled=True)
    arrival_dest = lax.all_gather(destination, "seq", tiled=True)
    my_pos = own_index * tok_dev + jnp.arange(tok_dev, dtype=jnp.int32)
    pick = (arrival_dest[None, :] == my_pos[:, None]).astype(projected.dtype)
    queries = jnp.dot(pick, everything[:, 0, :], preferred_element_type=jnp.float32)
    queries = queries.astype(projected.dtype).reshape(tok_dev, heads_here, HD)
    keys = everything[:, 1, :].reshape(tokens, heads_here, HD)
    values = everything[:, 2, :].reshape(tokens, heads_here, HD)
    scores = (
        jnp.einsum("qhd,khd->hqk", queries, keys, preferred_element_type=jnp.float32) * score_scale
    )
    bounds = jnp.cumsum(doc_lengths)
    key_block = arrival_dest // BLK
    key_doc = segment_of(arrival_dest, bounds)
    query_block = my_pos // BLK
    query_doc = segment_of(my_pos, bounds)
    same_doc = query_doc[:, None] == key_doc[None, :]
    window = jnp.zeros((tok_dev, tokens), jnp.int32)
    for step in (-1, 0, 1):
        near = (query_block + step) % blocks_all
        window = window + (key_block[None, :] == near[:, None]).astype(jnp.int32)
    window = jnp.where(same_doc, window, 0)
    chosen = random_blocks[query_block]
    drawn = jnp.zeros((tok_dev, tokens), jnp.int32)
    for r in range(chosen.shape[1]):
        drawn = drawn + (key_block[None, :] == chosen[:, r][:, None]).astype(jnp.int32)
    glob_start = global_owner[0] * tok_dev
    in_glob = (arrival_dest >= glob_start) & (arrival_dest < glob_start + tok_dev)
    count = window + drawn + in_glob[None, :].astype(jnp.int32)
    live = count > 0
    near_scores = jnp.where(live[None], scores, big_negative)
    row_peak = jnp.max(near_scores, axis=2)
    near_exp = jnp.exp(near_scores - row_peak[..., None])
    count_f = count.astype(jnp.float32)[None]
    denominator = jnp.sum(near_exp * count_f, axis=2)
    weighted = near_exp.astype(jnp.bfloat16).astype(jnp.float32) * count_f
    weight_hi = weighted.astype(jnp.bfloat16)
    weight_lo = (weighted - weight_hi.astype(jnp.float32)).astype(jnp.bfloat16)
    mixed_sum = jnp.einsum("hqk,khd->qhd", weight_hi, values, preferred_element_type=jnp.float32)
    mixed_sum = mixed_sum + jnp.einsum(
        "hqk,khd->qhd", weight_lo, values, preferred_element_type=jnp.float32
    )
    sparse = (mixed_sum / jnp.transpose(denominator)[..., None]).reshape(tok_dev, columns)
    sparse = sparse.astype(jnp.bfloat16)
    glob_peak = jnp.max(scores, axis=2)
    glob_exp = jnp.exp(scores - glob_peak[..., None])
    glob_total = jnp.sum(glob_exp, axis=2)
    glob_accum = jnp.einsum(
        "hqk,khd->qhd", glob_exp, values.astype(jnp.float32), precision=lax.Precision.HIGHEST
    )
    glob_out = (glob_accum / jnp.transpose(glob_total)[..., None]).reshape(tok_dev, columns)
    glob_out = glob_out.astype(jnp.bfloat16)
    attn_rows = jnp.where(own_index == global_owner[0], glob_out, sparse)
    return lax.psum_scatter(
        jnp.dot(attn_rows, out_weight, preferred_element_type=jnp.float32).astype(jnp.bfloat16),
        "head",
        scatter_dimension=0,
        tiled=True,
    )


GATHER_LIMIT = 16 * 2**20


def shards(projected, destination, doc_lengths, random_blocks, global_owner, out_weight):
    gathered_bytes = lax.axis_size("seq") * projected.size * projected.dtype.itemsize
    if gathered_bytes <= GATHER_LIMIT:
        return gathered_plan(
            projected, destination, doc_lengths, random_blocks, global_owner, out_weight
        )
    return shards_ring(projected, destination, doc_lengths, random_blocks, global_owner, out_weight)


def solution(mesh):
    in_specs = (P("seq", None, "head"), P("seq"), P(), P(), P(), P("head", None))
    out_specs = P(("seq", "head"), None)
    return jax.shard_map(shards, mesh=mesh, in_specs=in_specs, out_specs=out_specs, check_vma=False)
```

profile of v0, /device:TPU:0, one launch (start us, length us, event | category | flops | bytes accessed | tf_op | source)
XLA Modules:
  0.0 158.5 jit_solution(2768139149473016350)
XLA Ops:
  6.5 2.3 %copy.18 = bf16[128,3,1024]{0,2,1:T(8,128)(2,1)} copy(bf16[128,3,1024]{2,0,1:T(8,128)(2,1)} %param.6) | data formatting | bytes 1572864 | tf_op args[0]
  8.9 0.0 reduce-scatter.2.cloned.1.call-start
  10.2 0.8 copy.21
  11.0 0.8 reduce-window.8
  11.8 0.6 gather_fusion
  12.5 22.5 %all-gather = s32[8,1,128]{2,1,0:T(1,128)S(1)} all-gather(s32[1,1,128]{2,1,0:T(1,128)} %bitcast.59), channel_id=1, replica_groups=mesh['seq'=8,'head'=4] {'seq'}, dimensions={0}, use_global_device_ids=true | all-gather | bytes 4608 | tf_op jit(solution)/shard_map/all_gather | solution.py:187
  35.0 0.1 convert_reduce_fusion.1
  35.1 0.1 convert_reduce_fusion
  35.2 0.2 slice_reduce_fusion.2
  35.4 0.5 fusion.34
  35.9 0.5 fusion.33
  36.4 75.7 %all-gather.3.cloned.1.call-done = bf16[1024,3,1024]{0,2,1:T(8,128)(2,1)} async-done(((bf16[128,3,1024]{0,2,1:T(8,128)(2,1)}), bf16[1024,3,1024]{0,2,1:T(8,128)(2,1)}) %all-gather.3.cloned.1.call-update) | async-done | bytes 6291472 | tf_op jit(solution)/shard_map/all_gather | solution.py:186
  112.1 2.7 %fusion.49 = (bf16[1024,1,1024]{0,2,1:T(8,128)(2,1)S(1)}, bf16[1024,1,1024]{0,2,1:T(8,128)(2,1)S(1)}) fusion(bf16[1024,3,1024]{0,2,1:T(8,128)(2,1)} %all-gather.3.cloned.1.call-done), kind=kLoop, calls=%fused_computation.88 | loop fusion | bytes 8388608 | tf_op jit(solution)/shard_map/slice | solution.py:192
  114.8 2.4 %fusion.24 = bf16[16,8,8,128]{3,2,1,0:T(8,128)(2,1)S(1)} fusion(bf16[1024,3,1024]{0,2,1:T(8,128)(2,1)} %all-gather.3.cloned.1.call-done, s32[1024]{0:T(1024)S(1)} %bitcast.57, s32[128]{0:T(128)S(1)} %get-tuple-element.17), kind=kOutput, calls=%fused_computation.31 | convolution fusion | flops 268697600 | bytes 2363904 | tf_op jit(solution)/shard_map/dot_general | solution.py:190
  117.2 0.8 multiply_reduce_fusion.1
  118.0 0.9 fusion.2
  118.9 2.9 %fusion.31 = bf16[128,8,128]{0,2,1:T(8,128)(2,1)S(1)} fusion(bf16[1024,8,128]{0,2,1:T(8,128)(2,1)S(1)} %bitcast.49, f32[8,128,1024]{2,1,0:T(8,128)S(1)} %get-tuple-element.11, f32[8,128]{1,0:T(8,128)S(1)} %get-tuple-element.10, f32[128,8]{0,1:T(8,128)S(1)} %bitcast.58), kind=kOutput, calls=%fused_computation.38 | convolution fusion | flops 1612972032 | bytes 6561792 | tf_op jit(solution)/shard_map/hqk,khd->qhd/dot_general | solution.py:233
  121.8 2.2 %multiply_reduce_fusion = (f32[8,128]{1,0:T(8,128)S(1)}, bf16[8,128,1024]{2,1,0:T(8,128)(2,1)S(1)}) fusion(f32[128,1024]{1,0:T(8,128)S(1)} %fusion.33, f32[8,128,1024]{2,1,0:T(8,128)S(1)} %get-tuple-element.11, pred[128,1024]{1,0:T(8,128)(4,1)S(1)} %fusion.34), kind=kOutput, calls=%fused_computation.3 | output fusion | flops 8389631 | bytes 6950912 | tf_op jit(solution)/shard_map/sub | solution.py:218
  124.0 0.8 fusion.9
  124.8 1.0 fusion.29
  125.8 0.4 slice-done.1
  126.2 2.3 %convolution_convert_fusion = bf16[128,4096]{1,0:T(8,128)(2,1)} fusion(bf16[128,1024]{0,1:T(8,128)(2,1)S(1)} %bitcast.53, bf16[1024,4096]{1,0:T(8,128)(2,1)S(1)} %bitcast.48), kind=kOutput, calls=%fused_computation.2 | convolution fusion | flops 1074266112 | bytes 9699328 | tf_op jit(solution)/shard_map/dot_general | solution.py:240
  128.5 0.0 reduce-scatter.2.cloned.1.call-update
  128.5 23.2 %reduce-scatter.2.cloned.1.call-done = bf16[32,4096]{1,0:T(8,128)(2,1)} async-done(((bf16[128,4096]{1,0:T(8,128)(2,1)}), bf16[32,4096]{1,0:T(8,128)(2,1)}) %reduce-scatter.2.cloned.1.call-update) | async-done | bytes 262160 | tf_op jit(solution)/shard_map/reduce_scatter | solution.py:239
  (12 shorter events, 0.1 us)
Async XLA Ops:
  6.5 105.6 %all-gather.3.cloned.1.call-start = ((), (), s32[]{:S(2)}) async-start(), calls=%async_computation.1 | async-start | bytes 7077888 | tf_op jit(solution)/shard_map/all_gather | solution.py:186
  8.9 142.9 %reduce-scatter.2.cloned.1.call-start = ((), (), s32[]{:S(2)}) async-start(), calls=%async_computation.2 | async-start | bytes 1310720 | tf_op jit(solution)/shard_map/reduce_scatter | solution.py:239
  121.8 4.0 %slice-start = ((s8[8388608]{0:T(1024)(128)(4,1)}), s8[4194304]{0:T(1024)(128)(4,1)S(1)}, s32[]{:S(2)}) async-start(s8[8388608]{0:T(1024)(128)(4,1)} %bitcast.47), calls=%async_computation.3 | async-start | bytes 8388608
  124.0 2.2 %slice-start.1 = ((s8[8388608]{0:T(1024)(128)(4,1)}), s8[4194304]{0:T(1024)(128)(4,1)S(1)}, s32[]{:S(2)}) async-start(s8[8388608]{0:T(1024)(128)(4,1)} %bitcast.47), calls=%async_computation.4 | async-start | bytes 8388608
Sparse Core Ops, SparseCore 0:
  9.4 102.6 all-gather.2
  128.6 23.0 reduce-scatter.1
where the time goes:
time: 159 us
  waiting for transfers between devices  98.9 us (62%)
  blocking collectives  22.5 us (14%)
  between operations  14.8 us (9%)
  matrix products  10.2 us (6%)
  local copies, waits for them, and re-layouts  6.94 us (4%)
  other arithmetic  5.17 us (3%)
    all_gather x1, waiting for transfers between devices, gathered_plan(): everything = lax.all_gather(projected, 'seq', tiled=True)  75.7 us
    reduce_scatter x1, waiting for transfers between devices, gathered_plan(): lax.psum_scatter(jnp.dot(attn_rows, out_weight, preferred_element_type=jn...  23.2 us
    all_gather x1, blocking collectives, gathered_plan(): arrival_dest = lax.all_gather(destination, 'seq', tiled=True)  22.5 us
    unnamed x6, local copies, waits for them, and re-layouts  3.44 us
  transfers between devices with their start and end apart: 2, of which 2 were waited for; matrix products, arithmetic and copies ran while one was open for 2% of the time, Pallas kernels for 0%

commit v1 on v0

--- a/solution.py
+++ b/solution.py
@@ -183,7 +183,26 @@
     tokens = owners * tok_dev
     blocks_all = tokens // BLK
     score_scale = 1.0 / math.sqrt(HD)
-    everything = lax.all_gather(projected, "seq", tiled=True)
+    size, index, rows = (lax.axis_size("seq"), lax.axis_index("seq"), projected.shape[0])
+    forward = [(i_2, (i_2 + 1) % size) for i_2 in range(size)]
+    left = [(i_2, (i_2 - 1) % size) for i_2 in range(size)]
+    result = jnp.zeros(
+        (*projected.shape[:0], size * rows, *projected.shape[0 + 1 :]), projected.dtype
+    )
+    result = lax.dynamic_update_slice_in_dim(result, projected, index * rows, axis=0)
+    from_left = from_right = projected
+    middle = size // 2
+    for hop in range(1, middle + 1):
+        from_left = lax.ppermute(from_left, "seq", forward)
+        result = lax.dynamic_update_slice_in_dim(
+            result, from_left, (index - hop) % size * rows, axis=0
+        )
+        if hop < size - middle:
+            from_right = lax.ppermute(from_right, "seq", left)
+            result = lax.dynamic_update_slice_in_dim(
+                result, from_right, (index + hop) % size * rows, axis=0
+            )
+    everything = result
     arrival_dest = lax.all_gather(destination, "seq", tiled=True)
     my_pos = own_index * tok_dev + jnp.arange(tok_dev, dtype=jnp.int32)
     pick = (arrival_dest[None, :] == my_pos[:, None]).astype(projected.dtype)

time: 159 us -> 187 us (1.18)
  blocking collectives: 22.5 us -> 41.9 us
  starting transfers between devices: 0.04 us -> 18.2 us
  waiting for transfers between devices: 98.9 us -> 91.8 us
    all_gather x1 -> x0, waiting for transfers between devices: 75.7 us -> none  [gathered_plan(): everything = lax.all_gather(projected, 'seq', tiled=True)]
    ppermute x0 -> x7, waiting for transfers between devices: none -> 69.5 us  [the longest x4 69.5 us: gathered_plan(): from_left = lax.ppermute(from_left, 'seq', forward)]
    all_gather x1, blocking collectives: 22.5 us -> 41.9 us  [gathered_plan(): arrival_dest = lax.all_gather(destination, 'seq', tiled=True)]
    ppermute x0 -> x7, starting transfers between devices: none -> 18.2 us  [the longest x3 10.2 us: gathered_plan(): from_right = lax.ppermute(from_right, 'seq', left)]
    slice x1, local copies, waits for them, and re-layouts: 2.66 us -> 0.44 us  [gathered_plan(): keys = everything[:, 1, :].reshape(tokens, heads_here, HD)]
    dynamic_update_slice x0 -> x8, local copies, waits for them, and re-layouts: none -> 2.18 us  [the longest x4 1.08 us: gathered_plan(): lax.dynamic_update_slice_in_dim(result, from_left, (index - hop) % size *...]
  transfers between devices with their start and end apart: 2 -> 8, of which waited for: 2 -> 4; matrix products, arithmetic and copies ran while one was open for 2% -> 3% of each run, Pallas kernels for 0% -> 0%
where the time goes in v1:
time: 187 us
  waiting for transfers between devices  91.8 us (49%)
  blocking collectives  41.9 us (22%)
  starting transfers between devices  18.2 us (10%)
  between operations  14.9 us (8%)
  matrix products  8.34 us (4%)
  local copies, waits for them, and re-layouts  6.55 us (4%)
  other arithmetic  5.08 us (3%)
    ppermute x4, waiting for transfers between devices, gathered_plan(): from_left = lax.ppermute(from_left, 'seq', forward)  69.5 us
    all_gather x1, blocking collectives, gathered_plan(): arrival_dest = lax.all_gather(destination, 'seq', tiled=True)  41.9 us
    reduce_scatter x1, waiting for transfers between devices, gathered_plan(): lax.psum_scatter(jnp.dot(attn_rows, out_weight, preferred_element_type=jn...  22.3 us
    ppermute x3, starting transfers between devices, gathered_plan(): from_right = lax.ppermute(from_right, 'seq', left)  10.2 us
    ppermute x4, starting transfers between devices, gathered_plan(): from_left = lax.ppermute(from_left, 'seq', forward)  8.04 us
  transfers between devices with their start and end apart: 8, of which 4 were waited for; matrix products, arithmetic and copies ran while one was open for 3% of the time, Pallas kernels for 0%

profile of v1, /device:TPU:0, one launch (start us, length us, event | category | flops | bytes accessed | tf_op | source)
XLA Modules:
  0.0 186.8 jit_solution(12190818843260191830)
XLA Ops:
  6.5 1.5 copy.29
  8.1 3.0 %collective-permute-start = (bf16[128,3,1024]{0,2,1:T(8,128)(2,1)S(1)}, bf16[128,3,1024]{0,2,1:T(8,128)(2,1)S(1)}, u32[]{:S(2)}, u32[]{:S(2)}) collective-permute-start(bf16[128,3,1024]{0,2,1:T(8,128)(2,1)S(1)} %copy.29), channel_id=1, source_target_pairs={{0,4},{4,8},{8,12},{12,16},{16,20},{20,24},{24,28},{28,0},{1,5},{5... | collective-permute-start | bytes 2359304 | tf_op jit(solution)/shard_map/ppermute | solution.py:196
  11.1 3.1 %collective-permute-start.1 = (bf16[128,3,1024]{0,2,1:T(8,128)(2,1)S(1)}, bf16[128,3,1024]{0,2,1:T(8,128)(2,1)S(1)}, u32[]{:S(2)}, u32[]{:S(2)}) collective-permute-start(bf16[128,3,1024]{0,2,1:T(8,128)(2,1)S(1)} %copy.29), channel_id=1, source_target_pairs={{0,28},{4,0},{8,4},{12,8},{16,12},{20,16},{24,20},{28,24},{1,29},{... | collective-permute-start | bytes 2359304 | tf_op jit(solution)/shard_map/ppermute | solution.py:201
  15.5 0.8 copy.34
  16.3 0.8 reduce-window.8
  17.1 0.6 gather_fusion
  17.8 41.9 %all-gather = s32[8,1,128]{2,1,0:T(1,128)S(1)} all-gather(s32[1,1,128]{2,1,0:T(1,128)} %bitcast.59), channel_id=1, replica_groups=mesh['seq'=8,'head'=4] {'seq'}, dimensions={0}, use_global_device_ids=true | all-gather | bytes 4608 | tf_op jit(solution)/shard_map/all_gather | solution.py:206
  60.1 4.8 %collective-permute-start.3 = (bf16[128,3,1024]{0,2,1:T(8,128)(2,1)S(1)}, bf16[128,3,1024]{0,2,1:T(8,128)(2,1)S(1)}, u32[]{:S(2)}, u32[]{:S(2)}) collective-permute-start(bf16[128,3,1024]{0,2,1:T(8,128)(2,1)S(1)} %collective-permute-done.1), channel_id=1, source_target_pairs={{0,28},{4,0},{8,4},{12,8},{16,12},{20,16},{24,20},{28,24},{1,29},{... | collective-permute-start | bytes 2359304 | tf_op jit(solution)/shard_map/ppermute | solution.py:201
  64.9 25.2 %collective-permute-done.2 = bf16[128,3,1024]{0,2,1:T(8,128)(2,1)S(1)} collective-permute-done((bf16[128,3,1024]{0,2,1:T(8,128)(2,1)S(1)}, bf16[128,3,1024]{0,2,1:T(8,128)(2,1)S(1)}, u32[]{:S(2)}, u32[]{:S(2)}) %collective-permute-start.2) | collective-permute-done | bytes 786464 | tf_op jit(solution)/shard_map/ppermute | solution.py:196
  90.1 2.5 %collective-permute-start.4 = (bf16[128,3,1024]{0,2,1:T(8,128)(2,1)S(1)}, bf16[128,3,1024]{0,2,1:T(8,128)(2,1)S(1)}, u32[]{:S(2)}, u32[]{:S(2)}) collective-permute-start(bf16[128,3,1024]{0,2,1:T(8,128)(2,1)S(1)} %collective-permute-done.2), channel_id=1, source_target_pairs={{0,4},{4,8},{8,12},{12,16},{16,20},{20,24},{24,28},{28,0},{1,5},{5... | collective-permute-start | bytes 2359304 | tf_op jit(solution)/shard_map/ppermute | solution.py:196
  93.6 2.3 %collective-permute-start.5 = (bf16[128,3,1024]{0,2,1:T(8,128)(2,1)S(1)}, bf16[128,3,1024]{0,2,1:T(8,128)(2,1)S(1)}, u32[]{:S(2)}, u32[]{:S(2)}) collective-permute-start(bf16[128,3,1024]{0,2,1:T(8,128)(2,1)S(1)} %collective-permute-done.3), channel_id=1, source_target_pairs={{0,28},{4,0},{8,4},{12,8},{16,12},{20,16},{24,20},{28,24},{1,29},{... | collective-permute-start | bytes 2359304 | tf_op jit(solution)/shard_map/ppermute | solution.py:201
  95.9 0.8 broadcast_in_dim.13
  97.0 28.3 %collective-permute-done.4 = bf16[128,3,1024]{0,2,1:T(8,128)(2,1)S(1)} collective-permute-done((bf16[128,3,1024]{0,2,1:T(8,128)(2,1)S(1)}, bf16[128,3,1024]{0,2,1:T(8,128)(2,1)S(1)}, u32[]{:S(2)}, u32[]{:S(2)}) %collective-permute-start.4) | collective-permute-done | bytes 786464 | tf_op jit(solution)/shard_map/ppermute | solution.py:196
  125.3 2.5 %collective-permute-start.6 = (bf16[128,3,1024]{0,2,1:T(8,128)(2,1)S(1)}, bf16[128,3,1024]{0,2,1:T(8,128)(2,1)S(1)}, u32[]{:S(2)}, u32[]{:S(2)}) collective-permute-start(bf16[128,3,1024]{0,2,1:T(8,128)(2,1)S(1)} %collective-permute-done.4), channel_id=1, source_target_pairs={{0,4},{4,8},{8,12},{12,16},{16,20},{20,24},{24,28},{28,0},{1,5},{5... | collective-permute-start | bytes 2359304 | tf_op jit(solution)/shard_map/ppermute | solution.py:196
  129.5 16.0 %collective-permute-done.6 = bf16[128,3,1024]{0,2,1:T(8,128)(2,1)S(1)} collective-permute-done((bf16[128,3,1024]{0,2,1:T(8,128)(2,1)S(1)}, bf16[128,3,1024]{0,2,1:T(8,128)(2,1)S(1)}, u32[]{:S(2)}, u32[]{:S(2)}) %collective-permute-start.6) | collective-permute-done | bytes 786464 | tf_op jit(solution)/shard_map/ppermute | solution.py:196
  146.2 0.8 fusion.28
  147.1 0.8 multiply_reduce_fusion.1
  147.8 0.9 fusion.2
  148.7 2.1 %multiply_reduce_fusion = (f32[8,128]{1,0:T(8,128)S(1)}, bf16[8,128,1024]{2,1,0:T(8,128)(2,1)S(1)}) fusion(f32[128,1024]{1,0:T(8,128)S(1)} %fusion.43, f32[8,128,1024]{2,1,0:T(8,128)S(1)} %get-tuple-element.11, pred[128,1024]{1,0:T(8,128)(4,1)S(1)} %fusion.44), kind=kOutput, calls=%fused_computation.3 | output fusion | flops 8389631 | bytes 6950912 | tf_op jit(solution)/shard_map/sub | solution.py:237
  150.9 0.7 fusion.11
  151.6 2.8 %fusion.41 = bf16[128,8,128]{0,2,1:T(8,128)(2,1)S(1)} fusion(bf16[1024,8,128]{0,2,1:T(8,128)(2,1)S(1)} %bitcast.51, f32[8,128,1024]{2,1,0:T(8,128)S(1)} %get-tuple-element.11, f32[8,128]{1,0:T(8,128)S(1)} %get-tuple-element.10, f32[128,8]{0,1:T(8,128)S(1)} %bitcast.58), kind=kOutput, calls=%fused_computation.38 | convolution fusion | flops 1612972032 | bytes 6561792 | tf_op jit(solution)/shard_map/hqk,khd->qhd/dot_general | solution.py:252
  154.4 0.9 fusion.35
  155.4 2.3 %convolution_convert_fusion = bf16[128,4096]{1,0:T(8,128)(2,1)} fusion(bf16[128,1024]{0,1:T(8,128)(2,1)S(1)} %bitcast.53, bf16[1024,4096]{1,0:T(8,128)(2,1)S(1)} %bitcast.48), kind=kOutput, calls=%fused_computation.2 | convolution fusion | flops 1074266112 | bytes 9699328 | tf_op jit(solution)/shard_map/dot_general | solution.py:259
  157.7 22.3 %reduce-scatter.2.cloned.1.call-done = bf16[32,4096]{1,0:T(8,128)(2,1)} async-done(((bf16[128,4096]{1,0:T(8,128)(2,1)}), bf16[32,4096]{1,0:T(8,128)(2,1)}) %reduce-scatter.2.cloned.1.call-update) | async-done | bytes 262160 | tf_op jit(solution)/shard_map/reduce_scatter | solution.py:258
  (33 shorter events, 4.2 us)
Async XLA Ops:
  6.5 173.4 %reduce-scatter.2.cloned.1.call-start = ((), (), s32[]{:S(2)}) async-start(), calls=%async_computation.1 | async-start | bytes 1310720 | tf_op jit(solution)/shard_map/reduce_scatter | solution.py:258
  8.1 51.6 %collective-permute-start = (bf16[128,3,1024]{0,2,1:T(8,128)(2,1)S(1)}, bf16[128,3,1024]{0,2,1:T(8,128)(2,1)S(1)}, u32[]{:S(2)}, u32[]{:S(2)}) collective-permute-start(bf16[128,3,1024]{0,2,1:T(8,128)(2,1)S(1)} %copy.29), channel_id=1, source_target_pairs={{0,4},{4,8},{8,12},{12,16},{16,20},{20,24},{24,28},{28,0},{1,5},{5... | collective-permute-start | bytes 2359304 | tf_op jit(solution)/shard_map/ppermute | solution.py:196
  11.1 49.0 %collective-permute-start.1 = (bf16[128,3,1024]{0,2,1:T(8,128)(2,1)S(1)}, bf16[128,3,1024]{0,2,1:T(8,128)(2,1)S(1)}, u32[]{:S(2)}, u32[]{:S(2)}) collective-permute-start(bf16[128,3,1024]{0,2,1:T(8,128)(2,1)S(1)} %copy.29), channel_id=1, source_target_pairs={{0,28},{4,0},{8,4},{12,8},{16,12},{20,16},{24,20},{28,24},{1,29},{... | collective-permute-start | bytes 2359304 | tf_op jit(solution)/shard_map/ppermute | solution.py:201
  59.6 30.4 %collective-permute-start.2 = (bf16[128,3,1024]{0,2,1:T(8,128)(2,1)S(1)}, bf16[128,3,1024]{0,2,1:T(8,128)(2,1)S(1)}, u32[]{:S(2)}, u32[]{:S(2)}) collective-permute-start(bf16[128,3,1024]{0,2,1:T(8,128)(2,1)S(1)} %collective-permute-done), channel_id=1, source_target_pairs={{0,4},{4,8},{8,12},{12,16},{16,20},{20,24},{24,28},{28,0},{1,5},{5... | collective-permute-start | bytes 2359304 | tf_op jit(solution)/shard_map/ppermute | solution.py:196
  60.1 33.5 %collective-permute-start.3 = (bf16[128,3,1024]{0,2,1:T(8,128)(2,1)S(1)}, bf16[128,3,1024]{0,2,1:T(8,128)(2,1)S(1)}, u32[]{:S(2)}, u32[]{:S(2)}) collective-permute-start(bf16[128,3,1024]{0,2,1:T(8,128)(2,1)S(1)} %collective-permute-done.1), channel_id=1, source_target_pairs={{0,28},{4,0},{8,4},{12,8},{16,12},{20,16},{24,20},{28,24},{1,29},{... | collective-permute-start | bytes 2359304 | tf_op jit(solution)/shard_map/ppermute | solution.py:201
  90.1 35.2 %collective-permute-start.4 = (bf16[128,3,1024]{0,2,1:T(8,128)(2,1)S(1)}, bf16[128,3,1024]{0,2,1:T(8,128)(2,1)S(1)}, u32[]{:S(2)}, u32[]{:S(2)}) collective-permute-start(bf16[128,3,1024]{0,2,1:T(8,128)(2,1)S(1)} %collective-permute-done.2), channel_id=1, source_target_pairs={{0,4},{4,8},{8,12},{12,16},{16,20},{20,24},{24,28},{28,0},{1,5},{5... | collective-permute-start | bytes 2359304 | tf_op jit(solution)/shard_map/ppermute | solution.py:196
  93.6 35.6 %collective-permute-start.5 = (bf16[128,3,1024]{0,2,1:T(8,128)(2,1)S(1)}, bf16[128,3,1024]{0,2,1:T(8,128)(2,1)S(1)}, u32[]{:S(2)}, u32[]{:S(2)}) collective-permute-start(bf16[128,3,1024]{0,2,1:T(8,128)(2,1)S(1)} %collective-permute-done.3), channel_id=1, source_target_pairs={{0,28},{4,0},{8,4},{12,8},{16,12},{20,16},{24,20},{28,24},{1,29},{... | collective-permute-start | bytes 2359304 | tf_op jit(solution)/shard_map/ppermute | solution.py:201
  125.3 20.2 %collective-permute-start.6 = (bf16[128,3,1024]{0,2,1:T(8,128)(2,1)S(1)}, bf16[128,3,1024]{0,2,1:T(8,128)(2,1)S(1)}, u32[]{:S(2)}, u32[]{:S(2)}) collective-permute-start(bf16[128,3,1024]{0,2,1:T(8,128)(2,1)S(1)} %collective-permute-done.4), channel_id=1, source_target_pairs={{0,4},{4,8},{8,12},{12,16},{16,20},{20,24},{24,28},{28,0},{1,5},{5... | collective-permute-start | bytes 2359304 | tf_op jit(solution)/shard_map/ppermute | solution.py:196
  150.8 4.5 %slice-start = ((s8[8388608]{0:T(1024)(128)(4,1)}), s8[4194304]{0:T(1024)(128)(4,1)S(1)}, s32[]{:S(2)}) async-start(s8[8388608]{0:T(1024)(128)(4,1)} %bitcast.47), calls=%async_computation.2 | async-start | bytes 8388608
  151.6 3.8 %slice-start.1 = ((s8[8388608]{0:T(1024)(128)(4,1)}), s8[4194304]{0:T(1024)(128)(4,1)S(1)}, s32[]{:S(2)}) async-start(s8[8388608]{0:T(1024)(128)(4,1)} %bitcast.47), calls=%async_computation.3 | async-start | bytes 8388608
Sparse Core Ops, SparseCore 0:
  157.8 22.1 reduce-scatter.1
